TPU v7x, 512 devices: a whole 4x8x8 slice. The times are simulated.
512 devices in a mesh: dp: 4 (over y_lo, core), seq: 4 (over x), fsdp: 32 (over y_hi, z).
Axes of the slice: x: 4, y: 8 (y_hi: 4, y_lo: 2; y = y_hi * 2 + y_lo), z: 8, core: 2. Of those that a mesh axis runs over, the one named last changes fastest.
Arguments:
- patches: bfloat16 [128, 768, 6144], P(('dp', 'fsdp'), 'seq'), may hold values from -100 to 100
- segments: int32 [128, 768], P(('dp', 'fsdp'), 'seq'), may hold values from 0 to 7, never falling along the last dimension, each value on 1 to 384 neighbouring positions
- qkv_weight: bfloat16 [6144, 384], P('fsdp'), may hold values from -0.078125 to 0.078125
- cotangent: bfloat16 [128, 768, 128], P(('dp', 'fsdp'), 'seq'), may hold values from -6 to 6
Outputs:
- input_grad: bfloat16 [128, 768, 6144], P(('dp', 'fsdp'), 'seq')
- weight_grad: float32 [6144, 384], P('fsdp')
Inputs may be any that keep to these rules, and one draw needn't show every extreme that they name: `segments`: within a sequence the image number never falls; each of the 8 images has 1 to 384 patches and one has exactly 384.
All inputs are finite; a program needn't handle non-finite values.
Results may differ from a plain program's by a relative error of at most 0.034.
The roundings to bfloat16 on the way count: a program that leaves them out, or rounds other values in their place, can miss the bound.
Values may be sent and summed in bfloat16 or wider, within the bound.
No kernel may reach another device: no remote copies, remote signals or barrier semaphores. Data moves between devices by JAX's collectives and lax.ppermute only.
A program may use at most 64 MiB of HBM per device.

v0:
```python
import functools
import jax
import jax.numpy as jnp
from jax import lax
from jax.sharding import PartitionSpec as P


def contract_first(left, right):
    return lax.dot_general(
        left, right, (((0,), (0,)), ((), ())), preferred_element_type=jnp.float32
    )


def contract_last(left, right):
    return lax.dot_general(
        left, right, (((1,), (1,)), ((), ())), preferred_element_type=jnp.float32
    )


def dp_partner(x, bit):
    pairs = [(i, i ^ bit) for i in range(lax.axis_size("dp"))]
    return lax.ppermute(x, "dp", perm=pairs)


class Ring:

    def __init__(self, axis, size, inner):
        self.axis, self.size, self.inner = (axis, size, inner)

    def total(self):
        return lax.axis_size(self.axis)

    def position(self):
        return lax.axis_index(self.axis) // self.inner % self.size

    def shift(self, x, step):
        n, inner, total = (self.size, self.inner, self.total())
        pairs = []
        for i in range(total):
            pos = i // inner % n
            base = i - pos * inner
            pairs.append((i, base + (pos + step) % n * inner))
        return lax.ppermute(x, self.axis, perm=pairs)


def ring_gather(x, ring, beside=None, late=None):
    n = ring.size
    got, slot = ([x], {0: 0})
    cw, ccw = (x, x)
    last_cw = n - 1 if (n - 1) % 2 == 1 else n - 2
    last_ccw = n - 1 if (n - 1) % 2 == 0 else n - 2
    for t in range(1, n):
        if t % 2 == 1:
            cw = ring.shift(cw, 1)
            if t == 1 and beside is not None:
                cw, beside = lax.optimization_barrier((cw, beside))
            if t == last_cw and late is not None:
                cw, late = lax.optimization_barrier((cw, late))
            slot[(n - (t + 1) // 2) % n] = len(got)
            got.append(cw)
        else:
            ccw = ring.shift(ccw, -1)
            if t == last_ccw and late is not None:
                value, make = late
                ccw, value = lax.optimization_barrier((ccw, value))
                late = make(value)
            slot[t // 2] = len(got)
            got.append(ccw)
    if late is not None:
        return (jnp.stack(got), [slot[k] for k in range(n)], late)
    return (jnp.stack(got), [slot[k] for k in range(n)], beside)


def ring_reduce_scatter(blocks, ring, axis=0, beside=None):
    n = ring.size
    me = ring.position()

    def pick(index):
        return lax.dynamic_index_in_dim(blocks, index % n, axis=axis, keepdims=False)

    total = pick(me)
    if n == 1:
        return (total, beside)
    up, down = (n // 2, (n - 1) // 2)
    acc = pick(me + up)
    for t in range(1, up + 1):
        acc = ring.shift(acc.astype(jnp.bfloat16), 1)
        if t == 1 and beside is not None:
            acc, beside = lax.optimization_barrier((acc, beside))
        acc = acc.astype(jnp.float32)
        if t < up:
            acc = acc + pick(me + up - t)
    total = total + acc
    if down:
        acc = pick(me - down)
        for t in range(1, down + 1):
            acc = ring.shift(acc.astype(jnp.bfloat16), -1).astype(jnp.float32)
            if t < down:
                acc = acc + pick(me - down + t)
        total = total + acc
    return (total, beside)


def shards(patches, segments, qkv_weight, cotangent, inner_fsdp):
    features = patches[0]
    image_ids = segments[0]
    grad_out = cotangent[0]
    width_head = cotangent.shape[2]
    width_all = qkv_weight.shape[1]
    rows_w = qkv_weight.shape[0]
    half = width_all // 2
    scale = width_head ** (-0.5)
    core = lax.axis_index("dp") % 2
    first = core == 0
    outer_fsdp = lax.axis_size("fh")
    n_fsdp = outer_fsdp * inner_fsdp
    ring_y = Ring("fh", outer_fsdp, 1)
    ring_z = Ring("fz", inner_fsdp, 1)
    ring_x = Ring("seq", lax.axis_size("seq"), 1)
    w_mine = lax.dynamic_slice_in_dim(qkv_weight, core * half, half, axis=1)
    stack_y = lax.all_gather(w_mine, "fh", axis=0, tiled=False)
    relayout = lambda f: f.reshape(f.shape[0], outer_fsdp, inner_fsdp, rows_w)
    stack_zy, slot_z, blocked = ring_gather(stack_y, ring_z, late=(features, relayout))
    flat = stack_zy.reshape(-1, rows_w, half)
    me_y, me_z = (ring_y.position(), ring_z.position())
    absolute = jnp.arange(n_fsdp, dtype=jnp.int32)
    rel_z = (absolute % inner_fsdp - me_z) % inner_fsdp
    order = jnp.asarray(slot_z, jnp.int32)[rel_z] * outer_fsdp + absolute // inner_fsdp
    w_mine_all = jnp.take(flat, order, axis=0, mode="clip").reshape(n_fsdp * rows_w, half)
    w_other_all = dp_partner(w_mine_all, 1)
    h_mine = jnp.dot(features, w_mine_all, preferred_element_type=jnp.float32)
    h_other = jnp.dot(features, w_other_all, preferred_element_type=jnp.float32)
    projected = jnp.where(
        first,
        jnp.concatenate([h_mine, h_other], axis=1),
        jnp.concatenate([h_other, h_mine], axis=1),
    )
    heads = projected.astype(jnp.bfloat16)
    n_rows = features.shape[0]
    n_x = ring_x.size
    me_x = ring_x.position()
    ids_col = jnp.broadcast_to(image_ids.astype(jnp.bfloat16)[:, None], (n_rows, width_head))
    packed = jnp.concatenate([heads, grad_out, ids_col], axis=1)
    packed_all = lax.all_gather(packed, "seq", axis=0, tiled=True)
    query_all = packed_all[:, :width_head]
    keys_all = packed_all[:, width_head : 2 * width_head]
    values_all = packed_all[:, 2 * width_head : 3 * width_head]
    grad_out_all = packed_all[:, 3 * width_head : 4 * width_head]
    images_all = packed_all[:, 4 * width_head]
    scores = contract_last(query_all, keys_all) * scale
    allowed = images_all[:, None] == images_all[None, :]
    highest = jnp.max(jnp.where(allowed, scores, -jnp.inf), axis=1)
    summed = jnp.sum(jnp.where(allowed, jnp.exp(scores - highest[:, None]), 0.0), axis=1)
    log_total = highest + jnp.log(summed)
    attention = jnp.where(allowed, jnp.exp(scores - log_total[:, None]), 0.0)
    attention_low = attention.astype(jnp.bfloat16)
    output = jnp.dot(attention_low, values_all, preferred_element_type=jnp.float32)
    delta_rows = jnp.sum(grad_out_all.astype(jnp.float32) * output, axis=1)
    grad_attention = contract_last(grad_out_all, values_all)
    grad_scores = (attention * (grad_attention - delta_rows[:, None]) * scale).astype(jnp.bfloat16)
    start = me_x * n_rows
    own_rows = lax.dynamic_slice_in_dim(grad_scores, start, n_rows, axis=0)
    own_cols = lax.dynamic_slice_in_dim(grad_scores, start, n_rows, axis=1)
    own_attention = lax.dynamic_slice_in_dim(attention_low, start, n_rows, axis=1)
    grad_query = jnp.dot(own_rows, keys_all, preferred_element_type=jnp.float32)
    grad_key = contract_first(own_cols, query_all)
    grad_value = contract_first(own_attention, grad_out_all)
    grad_heads = jnp.concatenate([grad_query, grad_key, grad_value], axis=1).astype(jnp.bfloat16)
    g_lo = grad_heads[:, :half]
    g_hi = grad_heads[:, half:]
    g_mine = jnp.where(first, g_lo, g_hi)
    g_other = jnp.where(first, g_hi, g_lo)
    input_grad = (contract_last(g_mine, w_mine_all) + contract_last(g_other, w_other_all)).astype(
        jnp.bfloat16
    )
    wg_other = jnp.einsum("pyzd,pc->zydc", blocked, g_other, preferred_element_type=jnp.float32)
    wg_from_partner = dp_partner(wg_other.astype(jnp.bfloat16), 1)
    wg_mine = jnp.einsum("pyzd,pc->zydc", blocked, g_mine, preferred_element_type=jnp.float32)
    wg_mine, wg_from_partner = lax.optimization_barrier((wg_mine, wg_from_partner))
    blocks = wg_mine + wg_from_partner.astype(jnp.float32)
    over_z, input_grad = ring_reduce_scatter(blocks, ring_z, axis=0, beside=input_grad)
    over_fsdp, _ = ring_reduce_scatter(over_z, ring_y)
    by_seq = lax.all_gather(over_fsdp, "seq", axis=0, tiled=False)
    over_seq = by_seq[0]
    for s_i in range(1, by_seq.shape[0]):
        over_seq = over_seq + by_seq[s_i]
    by_dp = lax.all_gather(over_seq, "dp", axis=0, tiled=False)
    halves = []
    for c in range(2):
        part = by_dp[c]
        for d in range(c + 2, by_dp.shape[0], 2):
            part = part + by_dp[d]
        halves.append(part)
    weight_grad = jnp.concatenate(halves, axis=1)
    return (input_grad[None], weight_grad)


def inner_ring_size(mesh):
    axis = mesh.axis_names.index("fsdp")
    line = mesh.devices[tuple((0 if a != axis else slice(None) for a in range(mesh.devices.ndim)))]
    line = list(line)
    if not hasattr(line[0], "coords"):
        return len(line)
    count = 1
    while count < len(line) and line[count].coords[1] == line[0].coords[1]:
        count += 1
    return count


def solution(mesh):
    inner = inner_ring_size(mesh)
    sizes = dict(zip(mesh.axis_names, mesh.devices.shape))
    split = jax.sharding.Mesh(
        mesh.devices.reshape(sizes["dp"], sizes["seq"], sizes["fsdp"] // inner, inner),
        ("dp", "seq", "fh", "fz"),
    )
    rows = ("dp", "fh", "fz")
    placed = (P(rows, "seq", None), P(rows, "seq"), P(("fh", "fz"), None), P(rows, "seq", None))
    return jax.shard_map(
        functools.partial(shards, inner_fsdp=inner),
        mesh=split,
        in_specs=placed,
        out_specs=(P(rows, "seq", None), P(("fh", "fz"), None)),
        check_vma=False,
    )
```

profile of v0, /device:TPU:75, one launch (start us, length us, event | category | flops | bytes accessed | tf_op | source)
XLA Modules:
  0.0 222.7 jit_solution(9267431359710863556)
XLA Ops:
  1.6 13.7 %all-gather = bf16[768,192]{1,0:T(8,128)(2,1)S(1)} all-gather(bf16[192,192]{1,0:T(8,128)(2,1)S(1)} %constant_dynamic-slice_fusion), channel_id=2, replica_groups=mesh['dp'=4,'seq'=4,'fh'=4,'fz'=8] {'fh'}, dimensions={0}, use_global_device_ids=true | all-gather | bytes 368640 | tf_op jit(solution)/shard_map/all_gather | solution.py:121
  15.3 4.0 %collective-permute-start = (bf16[4,192,192]{2,1,0:T(8,128)(2,1)S(1)}, bf16[4,192,192]{2,1,0:T(8,128)(2,1)}, u32[]{:S(2)}, u32[]{:S(2)}) collective-permute-start(bf16[4,192,192]{2,1,0:T(8,128)(2,1)S(1)} %bitcast.108), channel_id=1, source_target_pairs={{0,1},{1,2},{2,3},{3,4},{4,5},{5,6},{6,7},{7,0},{8,9},{9,10},{10,1... | collective-permute-start | bytes 884744 | tf_op jit(solution)/shard_map/ppermute | solution.py:43
  24.0 4.0 %collective-permute-start.2 = (bf16[4,192,192]{2,1,0:T(8,128)(2,1)}, bf16[4,192,192]{2,1,0:T(8,128)(2,1)S(1)}, u32[]{:S(2)}, u32[]{:S(2)}) collective-permute-start(bf16[4,192,192]{2,1,0:T(8,128)(2,1)} %collective-permute-done), channel_id=1, source_target_pairs={{0,1},{1,2},{2,3},{3,4},{4,5},{5,6},{6,7},{7,0},{8,9},{9,10},{10,1... | collective-permute-start | bytes 884744 | tf_op jit(solution)/shard_map/ppermute | solution.py:43
  29.8 6.4 %collective-permute-start.3 = (bf16[4,192,192]{2,1,0:T(8,128)(2,1)S(1)}, bf16[4,192,192]{2,1,0:T(8,128)(2,1)S(1)}, u32[]{:S(2)}, u32[]{:S(2)}) collective-permute-start(bf16[4,192,192]{2,1,0:T(8,128)(2,1)S(1)} %collective-permute-done.1), channel_id=1, source_target_pairs={{0,7},{1,0},{2,1},{3,2},{4,3},{5,4},{6,5},{7,6},{8,15},{9,8},{10,9... | collective-permute-start | bytes 884744 | tf_op jit(solution)/shard_map/ppermute | solution.py:43
  40.9 4.6 %collective-permute-start.5 = (bf16[4,192,192]{2,1,0:T(8,128)(2,1)S(1)}, bf16[4,192,192]{2,1,0:T(8,128)(2,1)S(1)}, u32[]{:S(2)}, u32[]{:S(2)}) collective-permute-start(bf16[4,192,192]{2,1,0:T(8,128)(2,1)S(1)} %collective-permute-done.3), channel_id=1, source_target_pairs={{0,7},{1,0},{2,1},{3,2},{4,3},{5,4},{6,5},{7,6},{8,15},{9,8},{10,9... | collective-permute-start | bytes 884744 | tf_op jit(solution)/shard_map/ppermute | solution.py:43
  51.5 4.5 %reshape.141 = bf16[192,4,8,192]{3,2,1,0:T(8,128)(2,1)} reshape(bf16[192,6144]{1,0:T(8,128)(2,1)S(1)} %bitcast.105) | data formatting | bytes 4718592 | tf_op jit(solution)/shard_map/reshape | solution.py:122
  65.2 10.2 %collective-permute-start.7 = (bf16[6144,192]{0,1:T(8,128)(2,1)}, bf16[6144,192]{0,1:T(8,128)(2,1)}, u32[]{:S(2)}, u32[]{:S(2)}) collective-permute-start(bf16[6144,192]{0,1:T(8,128)(2,1)} %copy.31), channel_id=1, source_target_pairs={{0,128},{128,0},{256,384},{384,256},{1,129},{129,1},{257,385},{385... | collective-permute-start | bytes 7077896 | tf_op jit(solution)/shard_map/ppermute | solution.py:22
  82.7 12.4 %all_gather.21 = bf16[768,640]{1,0:T(8,128)(2,1)S(1)} all-gather(bf16[192,640]{1,0:T(8,128)(2,1)S(1)} %pad_maximum_fusion.1), channel_id=1, replica_groups=mesh['dp'=4,'seq'=4,'fh'=4,'fz'=8] {'seq'}, dimensions={0}, use_global_device_ids=true | all-gather | bytes 1228800 | tf_op jit(solution)/shard_map/all_gather | solution.py:144
  99.5 4.1 %convert_bitcast_fusion = bf16[8,4,192,192]{2,3,0,1:T(8,128)(2,1)} fusion(bf16[192,4,8,192]{3,2,1,0:T(8,128)(2,1)S(1)} %copy-done.1, pred[]{:T(512)S(6)} %eq.39, bf16[192,128]{1,0:T(8,128)(2,1)S(1)} %convolution_convert_fusion.1, bf16[192,128]{1,0:T(8,128)(2,1)S(1)} %convolution_convert_fusion.2, bf16[192,128]{1,0:T(8,128)(2,1)S(1)} %convolution_convert_fusion), kind=kOutput, calls=%fused_computation.8 | convolution fusion | flops 454496256 | bytes 4866049 | tf_op jit(solution)/shard_map/pyzd,pc->zydc/dot_general | solution.py:176
  103.6 5.4 %collective-permute-start.8 = (bf16[8,4,192,192]{2,3,0,1:T(8,128)(2,1)}, bf16[8,4,192,192]{2,3,0,1:T(8,128)(2,1)}, u32[]{:S(2)}, u32[]{:S(2)}) collective-permute-start(bf16[8,4,192,192]{2,3,0,1:T(8,128)(2,1)} %convert_bitcast_fusion), channel_id=1, source_target_pairs={{0,128},{128,0},{256,384},{384,256},{1,129},{129,1},{257,385},{385... | collective-permute-start | bytes 7077896 | tf_op jit(solution)/shard_map/ppermute | solution.py:22
  119.7 3.9 %fusion = bf16[192,6144]{1,0:T(8,128)(2,1)} fusion(f32[192,6144]{1,0:T(8,128)S(1)} %fusion.54, bf16[6144,192]{0,1:T(8,128)(2,1)} %collective-permute-done.7, pred[]{:T(512)S(6)} %eq.39, bf16[192,128]{1,0:T(8,128)(2,1)S(1)} %convolution_convert_fusion.1, bf16[192,128]{1,0:T(8,128)(2,1)S(1)} %convolution_convert_fusion.2, ...), kind=kOutput, calls=%fused_computation.3 | convolution fusion | flops 455675904 | bytes 9584641 | tf_op jit(solution)/shard_map/dot_general | solution.py:15
  123.6 4.7 %collective-permute-start.13 = (bf16[4,192,192]{1,2,0:T(8,128)(2,1)S(1)}, bf16[4,192,192]{1,2,0:T(8,128)(2,1)S(1)}, u32[]{:S(2)}, u32[]{:S(2)}) collective-permute-start(bf16[4,192,192]{1,2,0:T(8,128)(2,1)S(1)} %get-tuple-element.26), channel_id=1, source_target_pairs={{0,7},{1,0},{2,1},{3,2},{4,3},{5,4},{6,5},{7,6},{8,15},{9,8},{10,9... | collective-permute-start | bytes 884744 | tf_op jit(solution)/shard_map/ppermute | solution.py:43
  128.4 3.3 %collective-permute-done.9 = bf16[4,192,192]{1,2,0:T(8,128)(2,1)S(1)} collective-permute-done((bf16[4,192,192]{1,2,0:T(8,128)(2,1)S(1)}, bf16[4,192,192]{1,2,0:T(8,128)(2,1)S(1)}, u32[]{:S(2)}, u32[]{:S(2)}) %collective-permute-start.9) | collective-permute-done | bytes 294944 | tf_op jit(solution)/shard_map/ppermute | solution.py:43
  133.7 4.2 %collective-permute-done.13 = bf16[4,192,192]{1,2,0:T(8,128)(2,1)S(1)} collective-permute-done((bf16[4,192,192]{1,2,0:T(8,128)(2,1)S(1)}, bf16[4,192,192]{1,2,0:T(8,128)(2,1)S(1)}, u32[]{:S(2)}, u32[]{:S(2)}) %collective-permute-start.13) | collective-permute-done | bytes 294944 | tf_op jit(solution)/shard_map/ppermute | solution.py:43
  137.9 6.4 %collective-permute-done.10 = bf16[4,192,192]{1,2,0:T(8,128)(2,1)S(1)} collective-permute-done((bf16[4,192,192]{1,2,0:T(8,128)(2,1)S(1)}, bf16[4,192,192]{1,2,0:T(8,128)(2,1)S(1)}, u32[]{:S(2)}, u32[]{:S(2)}) %collective-permute-start.10) | collective-permute-done | bytes 294944 | tf_op jit(solution)/shard_map/ppermute | solution.py:43
  147.7 4.3 %collective-permute-start.14 = (bf16[4,192,192]{1,2,0:T(8,128)(2,1)S(1)}, bf16[4,192,192]{1,2,0:T(8,128)(2,1)S(1)}, u32[]{:S(2)}, u32[]{:S(2)}) collective-permute-start(bf16[4,192,192]{1,2,0:T(8,128)(2,1)S(1)} %get-tuple-element.25), channel_id=1, source_target_pairs={{0,7},{1,0},{2,1},{3,2},{4,3},{5,4},{6,5},{7,6},{8,15},{9,8},{10,9... | collective-permute-start | bytes 884744 | tf_op jit(solution)/shard_map/ppermute | solution.py:43
  152.1 5.3 %collective-permute-done.11 = bf16[4,192,192]{1,2,0:T(8,128)(2,1)S(1)} collective-permute-done((bf16[4,192,192]{1,2,0:T(8,128)(2,1)S(1)}, bf16[4,192,192]{1,2,0:T(8,128)(2,1)S(1)}, u32[]{:S(2)}, u32[]{:S(2)}) %collective-permute-start.11) | collective-permute-done | bytes 294944 | tf_op jit(solution)/shard_map/ppermute | solution.py:43
  159.8 5.2 %collective-permute-start.12 = (bf16[4,192,192]{1,2,0:T(8,128)(2,1)S(1)}, bf16[4,192,192]{1,2,0:T(8,128)(2,1)S(1)}, u32[]{:S(2)}, u32[]{:S(2)}) collective-permute-start(bf16[4,192,192]{1,2,0:T(8,128)(2,1)S(1)} %get-tuple-element.22), channel_id=1, source_target_pairs={{0,1},{1,2},{2,3},{3,4},{4,5},{5,6},{6,7},{7,0},{8,9},{9,10},{10,1... | collective-permute-start | bytes 884744 | tf_op jit(solution)/shard_map/ppermute | solution.py:43
  167.1 3.3 %collective-permute-done.12 = bf16[4,192,192]{1,2,0:T(8,128)(2,1)S(1)} collective-permute-done((bf16[4,192,192]{1,2,0:T(8,128)(2,1)S(1)}, bf16[4,192,192]{1,2,0:T(8,128)(2,1)S(1)}, u32[]{:S(2)}, u32[]{:S(2)}) %collective-permute-start.12) | collective-permute-done | bytes 294944 | tf_op jit(solution)/shard_map/ppermute | solution.py:43
  170.4 4.8 %collective-permute-done.15 = bf16[4,192,192]{1,2,0:T(8,128)(2,1)S(1)} collective-permute-done((bf16[4,192,192]{1,2,0:T(8,128)(2,1)S(1)}, bf16[4,192,192]{1,2,0:T(8,128)(2,1)S(1)}, u32[]{:S(2)}, u32[]{:S(2)}) %collective-permute-start.15) | collective-permute-done | bytes 294944 | tf_op jit(solution)/shard_map/ppermute | solution.py:43
  179.3 4.7 %collective-permute-start.18 = (bf16[192,192]{0,1:T(8,128)(2,1)S(1)}, bf16[192,192]{0,1:T(8,128)(2,1)S(1)}, u32[]{:S(2)}, u32[]{:S(2)}) collective-permute-start(bf16[192,192]{0,1:T(8,128)(2,1)S(1)} %get-tuple-element.31), channel_id=1, source_target_pairs={{0,24},{8,0},{16,8},{24,16},{1,25},{9,1},{17,9},{25,17},{2,26},{10... | collective-permute-start | bytes 221192 | tf_op jit(solution)/shard_map/ppermute | solution.py:43
  186.5 5.4 %collective-permute-done.17 = bf16[192,192]{0,1:T(8,128)(2,1)S(1)} collective-permute-done((bf16[192,192]{0,1:T(8,128)(2,1)S(1)}, bf16[192,192]{0,1:T(8,128)(2,1)S(1)}, u32[]{:S(2)}, u32[]{:S(2)}) %collective-permute-start.17) | collective-permute-done | bytes 73760 | tf_op jit(solution)/shard_map/ppermute | solution.py:43
  192.1 11.0 %all-gather.1 = f32[768,192]{1,0:T(8,128)S(1)} all-gather(f32[192,192]{1,0:T(8,128)S(1)} %copy.39), channel_id=3, replica_groups=mesh['dp'=4,'seq'=4,'fh'=4,'fz'=8] {'seq'}, dimensions={0}, use_global_device_ids=true | all-gather | bytes 737280 | tf_op jit(solution)/shard_map/all_gather | solution.py:183
  203.1 18.7 %all_gather.24 = f32[4,192,192]{2,1,0:T(8,128)S(1)} all-gather(f32[1,192,192]{2,1,0:T(8,128)S(1)} %fusion.28), channel_id=1, replica_groups=mesh['dp'=4,'seq'=4,'fh'=4,'fz'=8] {'dp'}, dimensions={0}, use_global_device_ids=true | all-gather | bytes 737280 | tf_op jit(solution)/shard_map/all_gather | solution.py:187
  (84 shorter events, 66.8 us)
Async XLA Ops:
  15.3 8.7 %collective-permute-start = (bf16[4,192,192]{2,1,0:T(8,128)(2,1)S(1)}, bf16[4,192,192]{2,1,0:T(8,128)(2,1)}, u32[]{:S(2)}, u32[]{:S(2)}) collective-permute-start(bf16[4,192,192]{2,1,0:T(8,128)(2,1)S(1)} %bitcast.108), channel_id=1, source_target_pairs={{0,1},{1,2},{2,3},{3,4},{4,5},{5,6},{6,7},{7,0},{8,9},{9,10},{10,1... | collective-permute-start | bytes 884744 | tf_op jit(solution)/shard_map/ppermute | solution.py:43
  19.3 10.5 %collective-permute-start.1 = (bf16[4,192,192]{2,1,0:T(8,128)(2,1)S(1)}, bf16[4,192,192]{2,1,0:T(8,128)(2,1)S(1)}, u32[]{:S(2)}, u32[]{:S(2)}) collective-permute-start(bf16[4,192,192]{2,1,0:T(8,128)(2,1)S(1)} %bitcast.109), channel_id=1, source_target_pairs={{0,7},{1,0},{2,1},{3,2},{4,3},{5,4},{6,5},{7,6},{8,15},{9,8},{10,9... | collective-permute-start | bytes 884744 | tf_op jit(solution)/shard_map/ppermute | solution.py:43
  22.1 29.4 %copy-start.4 = (bf16[1,192,6144]{2,1,0:T(8,128)(2,1)S(1)}, bf16[1,192,6144]{2,1,0:T(8,128)(2,1)}, u32[]{:S(2)}) copy-start(bf16[1,192,6144]{2,1,0:T(8,128)(2,1)} %param.5) | copy-start | bytes 7077892
  24.0 13.9 %collective-permute-start.2 = (bf16[4,192,192]{2,1,0:T(8,128)(2,1)}, bf16[4,192,192]{2,1,0:T(8,128)(2,1)S(1)}, u32[]{:S(2)}, u32[]{:S(2)}) collective-permute-start(bf16[4,192,192]{2,1,0:T(8,128)(2,1)} %collective-permute-done), channel_id=1, source_target_pairs={{0,1},{1,2},{2,3},{3,4},{4,5},{5,6},{6,7},{7,0},{8,9},{9,10},{10,1... | collective-permute-start | bytes 884744 | tf_op jit(solution)/shard_map/ppermute | solution.py:43
  29.8 11.1 %collective-permute-start.3 = (bf16[4,192,192]{2,1,0:T(8,128)(2,1)S(1)}, bf16[4,192,192]{2,1,0:T(8,128)(2,1)S(1)}, u32[]{:S(2)}, u32[]{:S(2)}) collective-permute-start(bf16[4,192,192]{2,1,0:T(8,128)(2,1)S(1)} %collective-permute-done.1), channel_id=1, source_target_pairs={{0,7},{1,0},{2,1},{3,2},{4,3},{5,4},{6,5},{7,6},{8,15},{9,8},{10,9... | collective-permute-start | bytes 884744 | tf_op jit(solution)/shard_map/ppermute | solution.py:43
  37.9 9.8 %collective-permute-start.4 = (bf16[4,192,192]{2,1,0:T(8,128)(2,1)S(1)}, bf16[4,192,192]{2,1,0:T(8,128)(2,1)}, u32[]{:S(2)}, u32[]{:S(2)}) collective-permute-start(bf16[4,192,192]{2,1,0:T(8,128)(2,1)S(1)} %collective-permute-done.2), channel_id=1, source_target_pairs={{0,1},{1,2},{2,3},{3,4},{4,5},{5,6},{6,7},{7,0},{8,9},{9,10},{10,1... | collective-permute-start | bytes 884744 | tf_op jit(solution)/shard_map/ppermute | solution.py:43
  40.9 10.5 %collective-permute-start.5 = (bf16[4,192,192]{2,1,0:T(8,128)(2,1)S(1)}, bf16[4,192,192]{2,1,0:T(8,128)(2,1)S(1)}, u32[]{:S(2)}, u32[]{:S(2)}) collective-permute-start(bf16[4,192,192]{2,1,0:T(8,128)(2,1)S(1)} %collective-permute-done.3), channel_id=1, source_target_pairs={{0,7},{1,0},{2,1},{3,2},{4,3},{5,4},{6,5},{7,6},{8,15},{9,8},{10,9... | collective-permute-start | bytes 884744 | tf_op jit(solution)/shard_map/ppermute | solution.py:43
  47.7 10.5 %collective-permute-start.6 = (bf16[4,192,192]{2,1,0:T(8,128)(2,1)}, bf16[4,192,192]{2,1,0:T(8,128)(2,1)}, u32[]{:S(2)}, u32[]{:S(2)}) collective-permute-start(bf16[4,192,192]{2,1,0:T(8,128)(2,1)} %collective-permute-done.4), channel_id=1, source_target_pairs={{0,1},{1,2},{2,3},{3,4},{4,5},{5,6},{6,7},{7,0},{8,9},{9,10},{10,1... | collective-permute-start | bytes 884744 | tf_op jit(solution)/shard_map/ppermute | solution.py:43
  62.6 12.8 %copy-start.7 = (s32[1,192]{1,0:T(1,128)S(1)}, s32[1,192]{1,0:T(1,128)}, u32[]{:S(2)}) copy-start(s32[1,192]{1,0:T(1,128)} %param.6) | copy-start | bytes 2308
  65.2 14.7 %collective-permute-start.7 = (bf16[6144,192]{0,1:T(8,128)(2,1)}, bf16[6144,192]{0,1:T(8,128)(2,1)}, u32[]{:S(2)}, u32[]{:S(2)}) collective-permute-start(bf16[6144,192]{0,1:T(8,128)(2,1)} %copy.31), channel_id=1, source_target_pairs={{0,128},{128,0},{256,384},{384,256},{1,129},{129,1},{257,385},{385... | collective-permute-start | bytes 7077896 | tf_op jit(solution)/shard_map/ppermute | solution.py:22
  75.5 4.4 %copy-start.5 = (bf16[1,192,6144]{2,1,0:T(8,128)(2,1)S(1)}, bf16[1,192,6144]{2,1,0:T(8,128)(2,1)}, u32[]{:S(2)}) copy-start(bf16[1,192,6144]{2,1,0:T(8,128)(2,1)} %param.5) | copy-start | bytes 7077892
  78.1 4.5 %copy-start.6 = (bf16[1,192,128]{2,1,0:T(8,128)(2,1)S(1)}, bf16[1,192,128]{2,1,0:T(8,128)(2,1)}, u32[]{:S(2)}) copy-start(bf16[1,192,128]{2,1,0:T(8,128)(2,1)} %param.8) | copy-start | bytes 147460
  103.6 10.9 %collective-permute-start.8 = (bf16[8,4,192,192]{2,3,0,1:T(8,128)(2,1)}, bf16[8,4,192,192]{2,3,0,1:T(8,128)(2,1)}, u32[]{:S(2)}, u32[]{:S(2)}) collective-permute-start(bf16[8,4,192,192]{2,3,0,1:T(8,128)(2,1)} %convert_bitcast_fusion), channel_id=1, source_target_pairs={{0,128},{128,0},{256,384},{384,256},{1,129},{129,1},{257,385},{385... | collective-permute-start | bytes 7077896 | tf_op jit(solution)/shard_map/ppermute | solution.py:22
  117.5 14.1 %copy-start.3 = (f32[8,4,192,192]{2,3,0,1:T(8,128)}, f32[8,4,192,192]{2,3,0,1:T(8,128)S(1)}, u32[]{:S(2)}) copy-start(f32[8,4,192,192]{2,3,0,1:T(8,128)S(1)} %convert_add_fusion) | copy-start | bytes 14155780
  117.6 14.0 %collective-permute-start.9 = (bf16[4,192,192]{1,2,0:T(8,128)(2,1)S(1)}, bf16[4,192,192]{1,2,0:T(8,128)(2,1)S(1)}, u32[]{:S(2)}, u32[]{:S(2)}) collective-permute-start(bf16[4,192,192]{1,2,0:T(8,128)(2,1)S(1)} %get-tuple-element.27), channel_id=1, source_target_pairs={{0,1},{1,2},{2,3},{3,4},{4,5},{5,6},{6,7},{7,0},{8,9},{9,10},{10,1... | collective-permute-start | bytes 884744 | tf_op jit(solution)/shard_map/ppermute | solution.py:43
  123.6 14.3 %collective-permute-start.13 = (bf16[4,192,192]{1,2,0:T(8,128)(2,1)S(1)}, bf16[4,192,192]{1,2,0:T(8,128)(2,1)S(1)}, u32[]{:S(2)}, u32[]{:S(2)}) collective-permute-start(bf16[4,192,192]{1,2,0:T(8,128)(2,1)S(1)} %get-tuple-element.26), channel_id=1, source_target_pairs={{0,7},{1,0},{2,1},{3,2},{4,3},{5,4},{6,5},{7,6},{8,15},{9,8},{10,9... | collective-permute-start | bytes 884744 | tf_op jit(solution)/shard_map/ppermute | solution.py:43
  131.8 12.5 %collective-permute-start.10 = (bf16[4,192,192]{1,2,0:T(8,128)(2,1)S(1)}, bf16[4,192,192]{1,2,0:T(8,128)(2,1)S(1)}, u32[]{:S(2)}, u32[]{:S(2)}) collective-permute-start(bf16[4,192,192]{1,2,0:T(8,128)(2,1)S(1)} %fusion.18), channel_id=1, source_target_pairs={{0,1},{1,2},{2,3},{3,4},{4,5},{5,6},{6,7},{7,0},{8,9},{9,10},{10,1... | collective-permute-start | bytes 884744 | tf_op jit(solution)/shard_map/ppermute | solution.py:43
  145.8 11.6 %collective-permute-start.11 = (bf16[4,192,192]{1,2,0:T(8,128)(2,1)S(1)}, bf16[4,192,192]{1,2,0:T(8,128)(2,1)S(1)}, u32[]{:S(2)}, u32[]{:S(2)}) collective-permute-start(bf16[4,192,192]{1,2,0:T(8,128)(2,1)S(1)} %get-tuple-element.24), channel_id=1, source_target_pairs={{0,1},{1,2},{2,3},{3,4},{4,5},{5,6},{6,7},{7,0},{8,9},{9,10},{10,1... | collective-permute-start | bytes 884744 | tf_op jit(solution)/shard_map/ppermute | solution.py:43
  147.7 10.5 %collective-permute-start.14 = (bf16[4,192,192]{1,2,0:T(8,128)(2,1)S(1)}, bf16[4,192,192]{1,2,0:T(8,128)(2,1)S(1)}, u32[]{:S(2)}, u32[]{:S(2)}) collective-permute-start(bf16[4,192,192]{1,2,0:T(8,128)(2,1)S(1)} %get-tuple-element.25), channel_id=1, source_target_pairs={{0,7},{1,0},{2,1},{3,2},{4,3},{5,4},{6,5},{7,6},{8,15},{9,8},{10,9... | collective-permute-start | bytes 884744 | tf_op jit(solution)/shard_map/ppermute | solution.py:43
  159.8 10.6 %collective-permute-start.12 = (bf16[4,192,192]{1,2,0:T(8,128)(2,1)S(1)}, bf16[4,192,192]{1,2,0:T(8,128)(2,1)S(1)}, u32[]{:S(2)}, u32[]{:S(2)}) collective-permute-start(bf16[4,192,192]{1,2,0:T(8,128)(2,1)S(1)} %get-tuple-element.22), channel_id=1, source_target_pairs={{0,1},{1,2},{2,3},{3,4},{4,5},{5,6},{6,7},{7,0},{8,9},{9,10},{10,1... | collective-permute-start | bytes 884744 | tf_op jit(solution)/shard_map/ppermute | solution.py:43
  165.1 10.1 %collective-permute-start.15 = (bf16[4,192,192]{1,2,0:T(8,128)(2,1)S(1)}, bf16[4,192,192]{1,2,0:T(8,128)(2,1)S(1)}, u32[]{:S(2)}, u32[]{:S(2)}) collective-permute-start(bf16[4,192,192]{1,2,0:T(8,128)(2,1)S(1)} %get-tuple-element.23), channel_id=1, source_target_pairs={{0,7},{1,0},{2,1},{3,2},{4,3},{5,4},{6,5},{7,6},{8,15},{9,8},{10,9... | collective-permute-start | bytes 884744 | tf_op jit(solution)/shard_map/ppermute | solution.py:43
  176.5 7.5 %collective-permute-start.16 = (bf16[192,192]{0,1:T(8,128)(2,1)S(1)}, bf16[192,192]{0,1:T(8,128)(2,1)S(1)}, u32[]{:S(2)}, u32[]{:S(2)}) collective-permute-start(bf16[192,192]{0,1:T(8,128)(2,1)S(1)} %get-tuple-element.30), channel_id=1, source_target_pairs={{0,8},{8,16},{16,24},{24,0},{1,9},{9,17},{17,25},{25,1},{2,10},{10... | collective-permute-start | bytes 221192 | tf_op jit(solution)/shard_map/ppermute | solution.py:43
  179.3 7.2 %collective-permute-start.18 = (bf16[192,192]{0,1:T(8,128)(2,1)S(1)}, bf16[192,192]{0,1:T(8,128)(2,1)S(1)}, u32[]{:S(2)}, u32[]{:S(2)}) collective-permute-start(bf16[192,192]{0,1:T(8,128)(2,1)S(1)} %get-tuple-element.31), channel_id=1, source_target_pairs={{0,24},{8,0},{16,8},{24,16},{1,25},{9,1},{17,9},{25,17},{2,26},{10... | collective-permute-start | bytes 221192 | tf_op jit(solution)/shard_map/ppermute | solution.py:43
  184.0 7.9 %collective-permute-start.17 = (bf16[192,192]{0,1:T(8,128)(2,1)S(1)}, bf16[192,192]{0,1:T(8,128)(2,1)S(1)}, u32[]{:S(2)}, u32[]{:S(2)}) collective-permute-start(bf16[192,192]{0,1:T(8,128)(2,1)S(1)} %fusion.29), channel_id=1, source_target_pairs={{0,8},{8,16},{16,24},{24,0},{1,9},{9,17},{17,25},{25,1},{2,10},{10... | collective-permute-start | bytes 221192 | tf_op jit(solution)/shard_map/ppermute | solution.py:43
  (3 other events, 4.7 us)
where the time goes:
time: 224 us; the launch traced here: 223 us
  starting transfers between devices  71.7 us (32%)
  blocking collectives  55.8 us (25%)
  waiting for transfers between devices  41.5 us (19%)
  local copies, waits for them, and re-layouts  23.1 us (10%)
  matrix products  19.5 us (9%)
  other arithmetic  9.77 us (4%)
    ppermute x17, starting transfers between devices, shift(): return lax.ppermute(x, self.axis, perm=pairs)  56.1 us
    ppermute x17, waiting for transfers between devices, shift(): return lax.ppermute(x, self.axis, perm=pairs)  38.6 us
    all_gather x1, blocking collectives, shards(): by_dp = lax.all_gather(over_seq, 'dp', axis=0, tiled=False)  18.7 us
    ppermute x2, starting transfers between devices, dp_partner(): return lax.ppermute(x, 'dp', perm=pairs)  15.6 us
    all_gather x1, blocking collectives, shards(): stack_y = lax.all_gather(w_mine, 'fh', axis=0, tiled=False)  13.7 us
    all_gather x1, blocking collectives, shards(): packed_all = lax.all_gather(packed, 'seq', axis=0, tiled=True)  12.4 us
    all_gather x1, blocking collectives, shards(): by_seq = lax.all_gather(over_fsdp, 'seq', axis=0, tiled=False)  11 us
    unnamed x23, local copies, waits for them, and re-layouts  9.48 us
  transfers between devices with their start and end apart: 19, of which 16 were waited for; matrix products, arithmetic and copies ran while one was open for 11% of the time, Pallas kernels for 0%

commit v1 on v0

--- a/solution.py
+++ b/solution.py
@@ -141,7 +141,9 @@
     me_x = ring_x.position()
     ids_col = jnp.broadcast_to(image_ids.astype(jnp.bfloat16)[:, None], (n_rows, width_head))
     packed = jnp.concatenate([heads, grad_out, ids_col], axis=1)
-    packed_all = lax.all_gather(packed, "seq", axis=0, tiled=True)
+    packed_all = jnp.concatenate(
+        lax.all_to_all(jnp.stack([packed] * lax.axis_size("seq")), "seq", 0, 0), axis=0
+    )
     query_all = packed_all[:, :width_head]
     keys_all = packed_all[:, width_head : 2 * width_head]
     values_all = packed_all[:, 2 * width_head : 3 * width_head]

time: 224 us -> 241 us (1.076)
  the two profiles are of different devices: /device:TPU:75 before, /device:TPU:1 now
where the time goes in v1:
time: 241 us; the launch traced here: 239 us
  starting transfers between devices  76.6 us (32%)
  waiting for transfers between devices  53.4 us (22%)
  blocking collectives  43.3 us (18%)
  local copies, waits for them, and re-layouts  27.3 us (11%)
  matrix products  26.6 us (11%)
  other arithmetic  10.8 us (4%)
    ppermute x17, starting transfers between devices, shift(): return lax.ppermute(x, self.axis, perm=pairs)  58.5 us
    ppermute x17, waiting for transfers between devices, shift(): return lax.ppermute(x, self.axis, perm=pairs)  36.4 us
    all_gather x1, blocking collectives, shards(): by_dp = lax.all_gather(over_seq, 'dp', axis=0, tiled=False)  16.3 us
    all_gather x1, blocking collectives, shards(): stack_y = lax.all_gather(w_mine, 'fh', axis=0, tiled=False)  16.3 us
    all_to_all x1, waiting for transfers between devices, shards(): lax.all_to_all(jnp.stack([packed] * lax.axis_size('seq')), 'seq', 0, 0)  14.1 us
    ppermute x2, starting transfers between devices, dp_partner(): return lax.ppermute(x, 'dp', perm=pairs)  13.8 us
    unnamed x27, local copies, waits for them, and re-layouts  11.7 us
    all_gather x1, blocking collectives, shards(): by_seq = lax.all_gather(over_fsdp, 'seq', axis=0, tiled=False)  10.7 us
  transfers between devices with their start and end apart: 20, of which 17 were waited for; matrix products, arithmetic and copies ran while one was open for 10% of the time, Pallas kernels for 0%

profile of v1, /device:TPU:1, one launch (start us, length us, event | category | flops | bytes accessed | tf_op | source)
XLA Modules:
  0.0 239.4 jit_solution(11142870628545131331)
XLA Ops:
  1.6 16.3 %all-gather = bf16[768,192]{1,0:T(8,128)(2,1)S(1)} all-gather(bf16[192,192]{1,0:T(8,128)(2,1)S(1)} %constant_dynamic-slice_fusion), channel_id=2, replica_groups=mesh['dp'=4,'seq'=4,'fh'=4,'fz'=8] {'fh'}, dimensions={0}, use_global_device_ids=true | all-gather | bytes 368640 | tf_op jit(solution)/shard_map/all_gather | solution.py:121
  17.9 3.2 %collective-permute-start = (bf16[4,192,192]{2,1,0:T(8,128)(2,1)S(1)}, bf16[4,192,192]{2,1,0:T(8,128)(2,1)}, u32[]{:S(2)}, u32[]{:S(2)}) collective-permute-start(bf16[4,192,192]{2,1,0:T(8,128)(2,1)S(1)} %bitcast.109), channel_id=1, source_target_pairs={{0,1},{1,2},{2,3},{3,4},{4,5},{5,6},{6,7},{7,0},{8,9},{9,10},{10,1... | collective-permute-start | bytes 884744 | tf_op jit(solution)/shard_map/ppermute | solution.py:43
  21.2 8.6 %collective-permute-start.1 = (bf16[4,192,192]{2,1,0:T(8,128)(2,1)S(1)}, bf16[4,192,192]{2,1,0:T(8,128)(2,1)S(1)}, u32[]{:S(2)}, u32[]{:S(2)}) collective-permute-start(bf16[4,192,192]{2,1,0:T(8,128)(2,1)S(1)} %bitcast.110), channel_id=1, source_target_pairs={{0,7},{1,0},{2,1},{3,2},{4,3},{5,4},{6,5},{7,6},{8,15},{9,8},{10,9... | collective-permute-start | bytes 884744 | tf_op jit(solution)/shard_map/ppermute | solution.py:43
  36.8 4.6 %collective-permute-start.3 = (bf16[4,192,192]{2,1,0:T(8,128)(2,1)S(1)}, bf16[4,192,192]{2,1,0:T(8,128)(2,1)S(1)}, u32[]{:S(2)}, u32[]{:S(2)}) collective-permute-start(bf16[4,192,192]{2,1,0:T(8,128)(2,1)S(1)} %collective-permute-done.1), channel_id=1, source_target_pairs={{0,7},{1,0},{2,1},{3,2},{4,3},{5,4},{6,5},{7,6},{8,15},{9,8},{10,9... | collective-permute-start | bytes 884744 | tf_op jit(solution)/shard_map/ppermute | solution.py:43
  46.1 5.0 %collective-permute-start.5 = (bf16[4,192,192]{2,1,0:T(8,128)(2,1)S(1)}, bf16[4,192,192]{2,1,0:T(8,128)(2,1)S(1)}, u32[]{:S(2)}, u32[]{:S(2)}) collective-permute-start(bf16[4,192,192]{2,1,0:T(8,128)(2,1)S(1)} %collective-permute-done.3), channel_id=1, source_target_pairs={{0,7},{1,0},{2,1},{3,2},{4,3},{5,4},{6,5},{7,6},{8,15},{9,8},{10,9... | collective-permute-start | bytes 884744 | tf_op jit(solution)/shard_map/ppermute | solution.py:43
  56.8 4.5 %reshape.146 = bf16[192,4,8,192]{3,2,1,0:T(8,128)(2,1)} reshape(bf16[192,6144]{1,0:T(8,128)(2,1)S(1)} %bitcast.106) | data formatting | bytes 4718592 | tf_op jit(solution)/shard_map/reshape | solution.py:122
  71.1 10.5 %collective-permute-start.7 = (bf16[6144,192]{0,1:T(8,128)(2,1)}, bf16[6144,192]{0,1:T(8,128)(2,1)}, u32[]{:S(2)}, u32[]{:S(2)}) collective-permute-start(bf16[6144,192]{0,1:T(8,128)(2,1)} %copy.39), channel_id=1, source_target_pairs={{0,128},{128,0},{256,384},{384,256},{1,129},{129,1},{257,385},{385... | collective-permute-start | bytes 7077896 | tf_op jit(solution)/shard_map/ppermute | solution.py:22
  89.8 4.2 %all-to-all-start = ((bf16[4,192,640]{2,1,0:T(8,128)(2,1)}), bf16[4,192,640]{2,1,0:T(8,128)(2,1)}, u32[]{:S(2)}, u32[]{:S(2)}) async-start(bf16[4,192,640]{2,1,0:T(8,128)(2,1)} %stack.43), calls=%async_computation | async-start | bytes 1966080 | tf_op jit(solution)/shard_map/all_to_all | solution.py:145
  94.0 14.1 %all-to-all-done = bf16[4,192,640]{2,1,0:T(8,128)(2,1)} async-done(((bf16[4,192,640]{2,1,0:T(8,128)(2,1)}), bf16[4,192,640]{2,1,0:T(8,128)(2,1)}, u32[]{:S(2)}, u32[]{:S(2)}) %all-to-all-start) | async-done | bytes 983072 | tf_op jit(solution)/shard_map/all_to_all | solution.py:145
  123.9 4.1 %convert_bitcast_fusion = bf16[8,4,192,192]{2,3,0,1:T(8,128)(2,1)} fusion(bf16[192,4,8,192]{3,2,1,0:T(8,128)(2,1)S(1)} %copy-done.1, pred[]{:T(512)S(6)} %eq.39, bf16[192,128]{1,0:T(8,128)(2,1)S(1)} %convolution_convert_fusion.1, bf16[192,128]{1,0:T(8,128)(2,1)S(1)} %convolution_convert_fusion.2, bf16[192,128]{1,0:T(8,128)(2,1)S(1)} %convolution_convert_fusion), kind=kOutput, calls=%fused_computation.8 | convolution fusion | flops 454496256 | bytes 4866049 | tf_op jit(solution)/shard_map/pyzd,pc->zydc/dot_general | solution.py:178
  128.0 3.4 %collective-permute-start.8 = (bf16[8,4,192,192]{2,3,0,1:T(8,128)(2,1)}, bf16[8,4,192,192]{2,3,0,1:T(8,128)(2,1)}, u32[]{:S(2)}, u32[]{:S(2)}) collective-permute-start(bf16[8,4,192,192]{2,3,0,1:T(8,128)(2,1)} %convert_bitcast_fusion), channel_id=1, source_target_pairs={{0,128},{128,0},{256,384},{384,256},{1,129},{129,1},{257,385},{385... | collective-permute-start | bytes 7077896 | tf_op jit(solution)/shard_map/ppermute | solution.py:22
  136.8 3.0 %convert_add_fusion = f32[8,4,192,192]{2,3,0,1:T(8,128)S(1)} fusion(f32[8,4,192,192]{2,3,0,1:T(8,128)S(1)} %fusion.5, bf16[8,4,192,192]{2,3,0,1:T(8,128)(2,1)} %collective-permute-done.8), kind=kLoop, calls=%fused_computation.4 | loop fusion | flops 2359296 | bytes 11796480 | tf_op jit(solution)/shard_map/add | solution.py:182
  141.9 4.0 %fusion = bf16[192,6144]{1,0:T(8,128)(2,1)} fusion(f32[192,6144]{1,0:T(8,128)S(1)} %fusion.52, bf16[6144,192]{0,1:T(8,128)(2,1)} %collective-permute-done.7, pred[]{:T(512)S(6)} %eq.39, bf16[192,128]{1,0:T(8,128)(2,1)S(1)} %convolution_convert_fusion.1, bf16[192,128]{1,0:T(8,128)(2,1)S(1)} %convolution_convert_fusion.2, ...), kind=kOutput, calls=%fused_computation.3 | convolution fusion | flops 455675904 | bytes 9584641 | tf_op jit(solution)/shard_map/dot_general | solution.py:15
  145.9 4.5 %collective-permute-start.13 = (bf16[4,192,192]{1,2,0:T(8,128)(2,1)S(1)}, bf16[4,192,192]{1,2,0:T(8,128)(2,1)S(1)}, u32[]{:S(2)}, u32[]{:S(2)}) collective-permute-start(bf16[4,192,192]{1,2,0:T(8,128)(2,1)S(1)} %get-tuple-element.28), channel_id=1, source_target_pairs={{0,7},{1,0},{2,1},{3,2},{4,3},{5,4},{6,5},{7,6},{8,15},{9,8},{10,9... | collective-permute-start | bytes 884744 | tf_op jit(solution)/shard_map/ppermute | solution.py:43
  150.4 3.0 %collective-permute-done.9 = bf16[4,192,192]{1,2,0:T(8,128)(2,1)S(1)} collective-permute-done((bf16[4,192,192]{1,2,0:T(8,128)(2,1)S(1)}, bf16[4,192,192]{1,2,0:T(8,128)(2,1)S(1)}, u32[]{:S(2)}, u32[]{:S(2)}) %collective-permute-start.9) | collective-permute-done | bytes 294944 | tf_op jit(solution)/shard_map/ppermute | solution.py:43
  158.2 7.9 %collective-permute-done.10 = bf16[4,192,192]{1,2,0:T(8,128)(2,1)S(1)} collective-permute-done((bf16[4,192,192]{1,2,0:T(8,128)(2,1)S(1)}, bf16[4,192,192]{1,2,0:T(8,128)(2,1)S(1)}, u32[]{:S(2)}, u32[]{:S(2)}) %collective-permute-start.10) | collective-permute-done | bytes 294944 | tf_op jit(solution)/shard_map/ppermute | solution.py:43
  169.5 4.6 %collective-permute-start.14 = (bf16[4,192,192]{1,2,0:T(8,128)(2,1)S(1)}, bf16[4,192,192]{1,2,0:T(8,128)(2,1)S(1)}, u32[]{:S(2)}, u32[]{:S(2)}) collective-permute-start(bf16[4,192,192]{1,2,0:T(8,128)(2,1)S(1)} %get-tuple-element.27), channel_id=1, source_target_pairs={{0,7},{1,0},{2,1},{3,2},{4,3},{5,4},{6,5},{7,6},{8,15},{9,8},{10,9... | collective-permute-start | bytes 884744 | tf_op jit(solution)/shard_map/ppermute | solution.py:43
  174.1 5.0 %collective-permute-done.11 = bf16[4,192,192]{1,2,0:T(8,128)(2,1)S(1)} collective-permute-done((bf16[4,192,192]{1,2,0:T(8,128)(2,1)S(1)}, bf16[4,192,192]{1,2,0:T(8,128)(2,1)S(1)}, u32[]{:S(2)}, u32[]{:S(2)}) %collective-permute-start.11) | collective-permute-done | bytes 294944 | tf_op jit(solution)/shard_map/ppermute | solution.py:43
  183.6 5.3 %collective-permute-start.15 = (bf16[4,192,192]{1,2,0:T(8,128)(2,1)S(1)}, bf16[4,192,192]{1,2,0:T(8,128)(2,1)S(1)}, u32[]{:S(2)}, u32[]{:S(2)}) collective-permute-start(bf16[4,192,192]{1,2,0:T(8,128)(2,1)S(1)} %get-tuple-element.25), channel_id=1, source_target_pairs={{0,7},{1,0},{2,1},{3,2},{4,3},{5,4},{6,5},{7,6},{8,15},{9,8},{10,9... | collective-permute-start | bytes 884744 | tf_op jit(solution)/shard_map/ppermute | solution.py:43
  189.0 4.1 %collective-permute-done.12 = bf16[4,192,192]{1,2,0:T(8,128)(2,1)S(1)} collective-permute-done((bf16[4,192,192]{1,2,0:T(8,128)(2,1)S(1)}, bf16[4,192,192]{1,2,0:T(8,128)(2,1)S(1)}, u32[]{:S(2)}, u32[]{:S(2)}) %collective-permute-start.12) | collective-permute-done | bytes 294944 | tf_op jit(solution)/shard_map/ppermute | solution.py:43
  197.5 5.5 %collective-permute-start.18 = (bf16[192,192]{0,1:T(8,128)(2,1)S(1)}, bf16[192,192]{0,1:T(8,128)(2,1)S(1)}, u32[]{:S(2)}, u32[]{:S(2)}) collective-permute-start(bf16[192,192]{0,1:T(8,128)(2,1)S(1)} %get-tuple-element.33), channel_id=1, source_target_pairs={{0,24},{8,0},{16,8},{24,16},{1,25},{9,1},{17,9},{25,17},{2,26},{10... | collective-permute-start | bytes 221192 | tf_op jit(solution)/shard_map/ppermute | solution.py:43
  205.7 5.5 %collective-permute-done.17 = bf16[192,192]{0,1:T(8,128)(2,1)S(1)} collective-permute-done((bf16[192,192]{0,1:T(8,128)(2,1)S(1)}, bf16[192,192]{0,1:T(8,128)(2,1)S(1)}, u32[]{:S(2)}, u32[]{:S(2)}) %collective-permute-start.17) | collective-permute-done | bytes 73760 | tf_op jit(solution)/shard_map/ppermute | solution.py:43
  211.4 10.7 %all-gather.1 = f32[768,192]{1,0:T(8,128)S(1)} all-gather(f32[192,192]{1,0:T(8,128)S(1)} %copy.47), channel_id=3, replica_groups=mesh['dp'=4,'seq'=4,'fh'=4,'fz'=8] {'seq'}, dimensions={0}, use_global_device_ids=true | all-gather | bytes 737280 | tf_op jit(solution)/shard_map/all_gather | solution.py:185
  222.2 16.3 %all_gather.20 = f32[4,192,192]{2,1,0:T(8,128)S(1)} all-gather(f32[1,192,192]{2,1,0:T(8,128)S(1)} %fusion.28), channel_id=1, replica_groups=mesh['dp'=4,'seq'=4,'fh'=4,'fz'=8] {'dp'}, dimensions={0}, use_global_device_ids=true | all-gather | bytes 737280 | tf_op jit(solution)/shard_map/all_gather | solution.py:189
  (90 shorter events, 80.1 us)
Async XLA Ops:
  17.9 15.2 %collective-permute-start = (bf16[4,192,192]{2,1,0:T(8,128)(2,1)S(1)}, bf16[4,192,192]{2,1,0:T(8,128)(2,1)}, u32[]{:S(2)}, u32[]{:S(2)}) collective-permute-start(bf16[4,192,192]{2,1,0:T(8,128)(2,1)S(1)} %bitcast.109), channel_id=1, source_target_pairs={{0,1},{1,2},{2,3},{3,4},{4,5},{5,6},{6,7},{7,0},{8,9},{9,10},{10,1... | collective-permute-start | bytes 884744 | tf_op jit(solution)/shard_map/ppermute | solution.py:43
  21.2 15.6 %collective-permute-start.1 = (bf16[4,192,192]{2,1,0:T(8,128)(2,1)S(1)}, bf16[4,192,192]{2,1,0:T(8,128)(2,1)S(1)}, u32[]{:S(2)}, u32[]{:S(2)}) collective-permute-start(bf16[4,192,192]{2,1,0:T(8,128)(2,1)S(1)} %bitcast.110), channel_id=1, source_target_pairs={{0,7},{1,0},{2,1},{3,2},{4,3},{5,4},{6,5},{7,6},{8,15},{9,8},{10,9... | collective-permute-start | bytes 884744 | tf_op jit(solution)/shard_map/ppermute | solution.py:43
  30.5 26.2 %copy-start.4 = (bf16[1,192,6144]{2,1,0:T(8,128)(2,1)S(1)}, bf16[1,192,6144]{2,1,0:T(8,128)(2,1)}, u32[]{:S(2)}) copy-start(bf16[1,192,6144]{2,1,0:T(8,128)(2,1)} %param.5) | copy-start | bytes 7077892
  33.1 9.9 %collective-permute-start.2 = (bf16[4,192,192]{2,1,0:T(8,128)(2,1)}, bf16[4,192,192]{2,1,0:T(8,128)(2,1)S(1)}, u32[]{:S(2)}, u32[]{:S(2)}) collective-permute-start(bf16[4,192,192]{2,1,0:T(8,128)(2,1)} %collective-permute-done), channel_id=1, source_target_pairs={{0,1},{1,2},{2,3},{3,4},{4,5},{5,6},{6,7},{7,0},{8,9},{9,10},{10,1... | collective-permute-start | bytes 884744 | tf_op jit(solution)/shard_map/ppermute | solution.py:43
  36.8 9.3 %collective-permute-start.3 = (bf16[4,192,192]{2,1,0:T(8,128)(2,1)S(1)}, bf16[4,192,192]{2,1,0:T(8,128)(2,1)S(1)}, u32[]{:S(2)}, u32[]{:S(2)}) collective-permute-start(bf16[4,192,192]{2,1,0:T(8,128)(2,1)S(1)} %collective-permute-done.1), channel_id=1, source_target_pairs={{0,7},{1,0},{2,1},{3,2},{4,3},{5,4},{6,5},{7,6},{8,15},{9,8},{10,9... | collective-permute-start | bytes 884744 | tf_op jit(solution)/shard_map/ppermute | solution.py:43
  43.0 10.0 %collective-permute-start.4 = (bf16[4,192,192]{2,1,0:T(8,128)(2,1)S(1)}, bf16[4,192,192]{2,1,0:T(8,128)(2,1)}, u32[]{:S(2)}, u32[]{:S(2)}) collective-permute-start(bf16[4,192,192]{2,1,0:T(8,128)(2,1)S(1)} %collective-permute-done.2), channel_id=1, source_target_pairs={{0,1},{1,2},{2,3},{3,4},{4,5},{5,6},{6,7},{7,0},{8,9},{9,10},{10,1... | collective-permute-start | bytes 884744 | tf_op jit(solution)/shard_map/ppermute | solution.py:43
  46.1 10.7 %collective-permute-start.5 = (bf16[4,192,192]{2,1,0:T(8,128)(2,1)S(1)}, bf16[4,192,192]{2,1,0:T(8,128)(2,1)S(1)}, u32[]{:S(2)}, u32[]{:S(2)}) collective-permute-start(bf16[4,192,192]{2,1,0:T(8,128)(2,1)S(1)} %collective-permute-done.3), channel_id=1, source_target_pairs={{0,7},{1,0},{2,1},{3,2},{4,3},{5,4},{6,5},{7,6},{8,15},{9,8},{10,9... | collective-permute-start | bytes 884744 | tf_op jit(solution)/shard_map/ppermute | solution.py:43
  53.0 11.0 %collective-permute-start.6 = (bf16[4,192,192]{2,1,0:T(8,128)(2,1)}, bf16[4,192,192]{2,1,0:T(8,128)(2,1)}, u32[]{:S(2)}, u32[]{:S(2)}) collective-permute-start(bf16[4,192,192]{2,1,0:T(8,128)(2,1)} %collective-permute-done.4), channel_id=1, source_target_pairs={{0,1},{1,2},{2,3},{3,4},{4,5},{5,6},{6,7},{7,0},{8,9},{9,10},{10,1... | collective-permute-start | bytes 884744 | tf_op jit(solution)/shard_map/ppermute | solution.py:43
  68.5 13.1 %copy-start.8 = (s32[1,192]{1,0:T(1,128)S(1)}, s32[1,192]{1,0:T(1,128)}, u32[]{:S(2)}) copy-start(s32[1,192]{1,0:T(1,128)} %param.6) | copy-start | bytes 2308
  71.1 14.9 %collective-permute-start.7 = (bf16[6144,192]{0,1:T(8,128)(2,1)}, bf16[6144,192]{0,1:T(8,128)(2,1)}, u32[]{:S(2)}, u32[]{:S(2)}) collective-permute-start(bf16[6144,192]{0,1:T(8,128)(2,1)} %copy.39), channel_id=1, source_target_pairs={{0,128},{128,0},{256,384},{384,256},{1,129},{129,1},{257,385},{385... | collective-permute-start | bytes 7077896 | tf_op jit(solution)/shard_map/ppermute | solution.py:22
  89.8 18.3 %all-to-all-start = ((bf16[4,192,640]{2,1,0:T(8,128)(2,1)}), bf16[4,192,640]{2,1,0:T(8,128)(2,1)}, u32[]{:S(2)}, u32[]{:S(2)}) async-start(bf16[4,192,640]{2,1,0:T(8,128)(2,1)} %stack.43), calls=%async_computation | async-start | bytes 1966080 | tf_op jit(solution)/shard_map/all_to_all | solution.py:145
  118.5 5.4 %copy-start.1 = (bf16[192,4,8,192]{3,2,1,0:T(8,128)(2,1)S(1)}, bf16[192,4,8,192]{3,2,1,0:T(8,128)(2,1)}, u32[]{:S(2)}) copy-start(bf16[192,4,8,192]{3,2,1,0:T(8,128)(2,1)} %reshape.146) | copy-start | bytes 7077892
  128.0 8.8 %collective-permute-start.8 = (bf16[8,4,192,192]{2,3,0,1:T(8,128)(2,1)}, bf16[8,4,192,192]{2,3,0,1:T(8,128)(2,1)}, u32[]{:S(2)}, u32[]{:S(2)}) collective-permute-start(bf16[8,4,192,192]{2,3,0,1:T(8,128)(2,1)} %convert_bitcast_fusion), channel_id=1, source_target_pairs={{0,128},{128,0},{256,384},{384,256},{1,129},{129,1},{257,385},{385... | collective-permute-start | bytes 7077896 | tf_op jit(solution)/shard_map/ppermute | solution.py:22
  139.9 13.5 %copy-start.3 = (f32[8,4,192,192]{2,3,0,1:T(8,128)}, f32[8,4,192,192]{2,3,0,1:T(8,128)S(1)}, u32[]{:S(2)}) copy-start(f32[8,4,192,192]{2,3,0,1:T(8,128)S(1)} %convert_add_fusion) | copy-start | bytes 14155780
  140.0 13.4 %collective-permute-start.9 = (bf16[4,192,192]{1,2,0:T(8,128)(2,1)S(1)}, bf16[4,192,192]{1,2,0:T(8,128)(2,1)S(1)}, u32[]{:S(2)}, u32[]{:S(2)}) collective-permute-start(bf16[4,192,192]{1,2,0:T(8,128)(2,1)S(1)} %get-tuple-element.29), channel_id=1, source_target_pairs={{0,1},{1,2},{2,3},{3,4},{4,5},{5,6},{6,7},{7,0},{8,9},{9,10},{10,1... | collective-permute-start | bytes 884744 | tf_op jit(solution)/shard_map/ppermute | solution.py:43
  145.9 12.3 %collective-permute-start.13 = (bf16[4,192,192]{1,2,0:T(8,128)(2,1)S(1)}, bf16[4,192,192]{1,2,0:T(8,128)(2,1)S(1)}, u32[]{:S(2)}, u32[]{:S(2)}) collective-permute-start(bf16[4,192,192]{1,2,0:T(8,128)(2,1)S(1)} %get-tuple-element.28), channel_id=1, source_target_pairs={{0,7},{1,0},{2,1},{3,2},{4,3},{5,4},{6,5},{7,6},{8,15},{9,8},{10,9... | collective-permute-start | bytes 884744 | tf_op jit(solution)/shard_map/ppermute | solution.py:43
  153.5 12.5 %collective-permute-start.10 = (bf16[4,192,192]{1,2,0:T(8,128)(2,1)S(1)}, bf16[4,192,192]{1,2,0:T(8,128)(2,1)S(1)}, u32[]{:S(2)}, u32[]{:S(2)}) collective-permute-start(bf16[4,192,192]{1,2,0:T(8,128)(2,1)S(1)} %fusion.18), channel_id=1, source_target_pairs={{0,1},{1,2},{2,3},{3,4},{4,5},{5,6},{6,7},{7,0},{8,9},{9,10},{10,1... | collective-permute-start | bytes 884744 | tf_op jit(solution)/shard_map/ppermute | solution.py:43
  167.6 11.6 %collective-permute-start.11 = (bf16[4,192,192]{1,2,0:T(8,128)(2,1)S(1)}, bf16[4,192,192]{1,2,0:T(8,128)(2,1)S(1)}, u32[]{:S(2)}, u32[]{:S(2)}) collective-permute-start(bf16[4,192,192]{1,2,0:T(8,128)(2,1)S(1)} %get-tuple-element.26), channel_id=1, source_target_pairs={{0,1},{1,2},{2,3},{3,4},{4,5},{5,6},{6,7},{7,0},{8,9},{9,10},{10,1... | collective-permute-start | bytes 884744 | tf_op jit(solution)/shard_map/ppermute | solution.py:43
  169.5 10.6 %collective-permute-start.14 = (bf16[4,192,192]{1,2,0:T(8,128)(2,1)S(1)}, bf16[4,192,192]{1,2,0:T(8,128)(2,1)S(1)}, u32[]{:S(2)}, u32[]{:S(2)}) collective-permute-start(bf16[4,192,192]{1,2,0:T(8,128)(2,1)S(1)} %get-tuple-element.27), channel_id=1, source_target_pairs={{0,7},{1,0},{2,1},{3,2},{4,3},{5,4},{6,5},{7,6},{8,15},{9,8},{10,9... | collective-permute-start | bytes 884744 | tf_op jit(solution)/shard_map/ppermute | solution.py:43
  181.6 11.4 %collective-permute-start.12 = (bf16[4,192,192]{1,2,0:T(8,128)(2,1)S(1)}, bf16[4,192,192]{1,2,0:T(8,128)(2,1)S(1)}, u32[]{:S(2)}, u32[]{:S(2)}) collective-permute-start(bf16[4,192,192]{1,2,0:T(8,128)(2,1)S(1)} %get-tuple-element.24), channel_id=1, source_target_pairs={{0,1},{1,2},{2,3},{3,4},{4,5},{5,6},{6,7},{7,0},{8,9},{9,10},{10,1... | collective-permute-start | bytes 884744 | tf_op jit(solution)/shard_map/ppermute | solution.py:43
  183.6 10.7 %collective-permute-start.15 = (bf16[4,192,192]{1,2,0:T(8,128)(2,1)S(1)}, bf16[4,192,192]{1,2,0:T(8,128)(2,1)S(1)}, u32[]{:S(2)}, u32[]{:S(2)}) collective-permute-start(bf16[4,192,192]{1,2,0:T(8,128)(2,1)S(1)} %get-tuple-element.25), channel_id=1, source_target_pairs={{0,7},{1,0},{2,1},{3,2},{4,3},{5,4},{6,5},{7,6},{8,15},{9,8},{10,9... | collective-permute-start | bytes 884744 | tf_op jit(solution)/shard_map/ppermute | solution.py:43
  195.5 8.2 %collective-permute-start.16 = (bf16[192,192]{0,1:T(8,128)(2,1)S(1)}, bf16[192,192]{0,1:T(8,128)(2,1)S(1)}, u32[]{:S(2)}, u32[]{:S(2)}) collective-permute-start(bf16[192,192]{0,1:T(8,128)(2,1)S(1)} %get-tuple-element.32), channel_id=1, source_target_pairs={{0,8},{8,16},{16,24},{24,0},{1,9},{9,17},{17,25},{25,1},{2,10},{10... | collective-permute-start | bytes 221192 | tf_op jit(solution)/shard_map/ppermute | solution.py:43
  197.5 8.2 %collective-permute-start.18 = (bf16[192,192]{0,1:T(8,128)(2,1)S(1)}, bf16[192,192]{0,1:T(8,128)(2,1)S(1)}, u32[]{:S(2)}, u32[]{:S(2)}) collective-permute-start(bf16[192,192]{0,1:T(8,128)(2,1)S(1)} %get-tuple-element.33), channel_id=1, source_target_pairs={{0,24},{8,0},{16,8},{24,16},{1,25},{9,1},{17,9},{25,17},{2,26},{10... | collective-permute-start | bytes 221192 | tf_op jit(solution)/shard_map/ppermute | solution.py:43
  203.8 7.5 %collective-permute-start.17 = (bf16[192,192]{0,1:T(8,128)(2,1)S(1)}, bf16[192,192]{0,1:T(8,128)(2,1)S(1)}, u32[]{:S(2)}, u32[]{:S(2)}) collective-permute-start(bf16[192,192]{0,1:T(8,128)(2,1)S(1)} %fusion.29), channel_id=1, source_target_pairs={{0,8},{8,16},{16,24},{24,0},{1,9},{9,17},{17,25},{25,1},{2,10},{10... | collective-permute-start | bytes 221192 | tf_op jit(solution)/shard_map/ppermute | solution.py:43
  (5 other events, 13.2 us)
